TPU v7x, 128 devices: a whole 4x4x4 slice. The times are simulated.
128 devices in a mesh: req: 16 (over y, z), mlp: 8 (over x, core).
Axes of the slice: x: 4, y: 4, z: 4, core: 2. Of those that a mesh axis runs over, the one named last changes fastest.
Arguments:
- tokens: bfloat16 [32768, 1536], P(('req', 'mlp')), may hold values from -6 to 6
- attn_gain: float32 [1536], replicated, may hold values from 0.1 to 1.9
- w_query: bfloat16 [1536, 1536], replicated, may hold values from -0.15625 to 0.15625
- w_keyval: bfloat16 [1536, 256], replicated, may hold values from -0.15625 to 0.15625
- w_out: bfloat16 [1536, 1536], replicated, may hold values from -0.15625 to 0.15625
- ffn_gain: float32 [1536], replicated, may hold values from 0.1 to 1.9
- w_gate: bfloat16 [1536, 4608], P('req', 'mlp'), may hold values from -0.15625 to 0.15625
- w_up: bfloat16 [1536, 4608], P('req', 'mlp'), may hold values from -0.15625 to 0.15625
- w_down: bfloat16 [1536, 4608], P('req', 'mlp'), may hold values from -0.09375 to 0.09375
- prefix_kv: bfloat16 [2, 128, 512, 256], P(None, 'req'), may hold values from -60 to 60, as said below
- own_prefix: bfloat16 [16, 512, 256], P('req'), may hold values from -60 to 60, as said below
- leaf_parent: int32 [16], replicated, may hold values from 0 to 127
- node_parent: int32 [128], replicated, may hold values from 0 to 127
- seg_lengths: int32 [3, 128], replicated, may hold values from 1 to 512
Outputs:
- layer_out: bfloat16 [32768, 1536], P(('req', 'mlp'))
Inputs may be any that keep to these rules, and one draw needn't show every extreme that they name: `prefix_kv`: columns below 128 are keys, the rest values. `own_prefix`: columns below 128 are keys, the rest values.
All inputs are finite; a program needn't handle non-finite values.
Results may differ from a plain program's by a relative error of at most 0.018.
Values may be sent and summed in bfloat16 or wider, within the bound.
No kernel may reach another device: no remote copies, remote signals or barrier semaphores. Data moves between devices by JAX's collectives and lax.ppermute only.
A program may use at most 192 MiB of HBM per device.

v0:
```python
import jax
import jax.numpy as jnp
from jax import lax
from jax.sharding import PartitionSpec as P

HEADS = 12
HD = 128
WINDOW = 1024
EPS = 1e-06


def rms_scale(values, gain):
    wide = values.astype(jnp.float32)
    return wide * lax.rsqrt(jnp.mean(wide * wide, axis=-1, keepdims=True) + EPS) * gain


def rotate(values, where_at):
    half_dim = values.shape[-1] // 2
    freqs = 10000.0 ** (-jnp.arange(half_dim, dtype=jnp.float32) / half_dim)
    angles = where_at.astype(jnp.float32)[:, None] * freqs[None, :]
    cosine = jnp.cos(angles)[:, None, :]
    sine = jnp.sin(angles)[:, None, :]
    first = values[..., :half_dim]
    second = values[..., half_dim:]
    return jnp.concatenate([first * cosine - second * sine, first * sine + second * cosine], -1)


def attend(queries, piece, key_at, key_live, query_at):
    scores = jnp.einsum("thd,kd->thk", queries, piece[:, :HD], preferred_element_type=jnp.float32)
    spacing = query_at[:, None] - key_at[None, :]
    allowed = (key_live[None, :] & (spacing >= 0) & (spacing < WINDOW))[:, None, :]
    top = jnp.max(jnp.where(allowed, scores, -jnp.inf), axis=-1)
    safe_top = jnp.where(jnp.isfinite(top), top, 0.0)
    weights = jnp.where(allowed, jnp.exp(scores - safe_top[..., None]), 0.0)
    mixed = jnp.einsum(
        "thk,kd->thd",
        weights.astype(jnp.bfloat16),
        piece[:, HD:],
        preferred_element_type=jnp.float32,
    )
    return (top, jnp.sum(weights, axis=-1), mixed)


def combine(first, second):
    top = jnp.maximum(first[0], second[0])
    safe_top = jnp.where(jnp.isfinite(top), top, 0.0)
    scale_first = jnp.exp(first[0] - safe_top)
    scale_second = jnp.exp(second[0] - safe_top)
    denom = first[1] * scale_first + second[1] * scale_second
    mixed = first[2] * scale_first[..., None] + second[2] * scale_second[..., None]
    return (top, denom, mixed)


def body(
    tokens,
    attn_gain,
    w_query,
    w_keyval,
    w_out,
    ffn_gain,
    w_gate,
    w_up,
    w_down,
    prefix_kv,
    own_prefix,
    leaf_parent,
    node_parent,
    seg_lengths,
):
    tok_rows = tokens.shape[0]
    requests = lax.axis_size("req")
    mine = lax.axis_index("req")
    position_group = lax.axis_index("mlp")
    node_dev = prefix_kv.shape[1]
    seg_slot = prefix_kv.shape[2]
    leaf = leaf_parent[mine]
    upper = node_parent[leaf]
    len_zero = seg_lengths[0, upper]
    len_one = seg_lengths[1, leaf]
    len_two = seg_lengths[2, mine]
    total = len_zero + len_one + len_two
    query_at = total + position_group * tok_rows + jnp.arange(tok_rows, dtype=jnp.int32)
    normed = rms_scale(tokens, attn_gain).astype(jnp.bfloat16)
    query_full = jnp.dot(normed, w_query, preferred_element_type=jnp.float32).reshape(
        tok_rows, HEADS, HD
    )
    queries = (rotate(query_full, query_at) * HD ** (-0.5)).astype(jnp.bfloat16)
    keyval_full = jnp.dot(normed, w_keyval, preferred_element_type=jnp.float32)
    new_keys = rotate(keyval_full[:, None, :HD], query_at)[:, 0].astype(jnp.bfloat16)
    new_vals = keyval_full[:, HD:].astype(jnp.bfloat16)
    new_keyval = jnp.concatenate([new_keys, new_vals], 1)
    start_state = (
        jnp.full((tok_rows, HEADS), -jnp.inf, jnp.float32),
        jnp.zeros((tok_rows, HEADS), jnp.float32),
        jnp.zeros((tok_rows, HEADS, HD), jnp.float32),
    )
    piece = lax.all_gather(new_keyval, "mlp", axis=0, tiled=True)
    piece_at = total + jnp.arange(piece.shape[0], dtype=jnp.int32)
    live = jnp.ones((piece.shape[0],), dtype=bool)
    own_state = combine(start_state, attend(queries, piece, piece_at, live, query_at))
    level_zero = node_parent[leaf_parent]
    wanted = jnp.stack([level_zero, leaf_parent], 1)
    owned = wanted // node_dev == mine
    local_slot = wanted % node_dev
    picker = (
        (local_slot[:, :, None] == jnp.arange(node_dev, dtype=jnp.int32)[None, None, :])
        & owned[:, :, None]
    ).astype(jnp.bfloat16)
    owners = wanted[mine] // node_dev
    from_owner = (jnp.arange(requests, dtype=jnp.int32)[:, None] == owners[None, :]).astype(
        jnp.bfloat16
    )
    outgoing = jnp.einsum(
        "rln,lnsc->rlsc", picker, prefix_kv, preferred_element_type=jnp.float32
    ).astype(jnp.bfloat16)
    arrived = lax.all_to_all(outgoing, "req", split_axis=0, concat_axis=0, tiled=True)
    levels = jnp.einsum(
        "rl,rlsc->lsc", from_owner, arrived, preferred_element_type=jnp.float32
    ).astype(jnp.bfloat16)
    offsets = jnp.arange(seg_slot, dtype=jnp.int32)
    cached = jnp.concatenate([levels[0], levels[1], own_prefix[0]], 0)
    cached_at = jnp.concatenate([offsets, len_zero + offsets, len_zero + len_one + offsets], 0)
    cached_live = jnp.concatenate([offsets < len_zero, offsets < len_one, offsets < len_two], 0)
    merged = combine(own_state, attend(queries, cached, cached_at, cached_live, query_at))
    context = (merged[2] / merged[1][..., None]).reshape(tok_rows, HEADS * HD).astype(jnp.bfloat16)
    attn_out = jnp.dot(context, w_out, preferred_element_type=jnp.float32)
    resid = (tokens.astype(jnp.float32) + attn_out).astype(jnp.bfloat16)
    ffn_in = rms_scale(resid, ffn_gain).astype(jnp.bfloat16)
    all_rows = lax.all_gather(ffn_in, "mlp", axis=0, tiled=True)
    gate_full, up_full, down_full = (
        lax.all_gather(w_gate, "req", axis=0, tiled=True),
        lax.all_gather(w_up, "req", axis=0, tiled=True),
        lax.all_gather(w_down, "req", axis=0, tiled=True),
    )
    gate = jnp.dot(all_rows, gate_full, preferred_element_type=jnp.float32)
    upward = jnp.dot(all_rows, up_full, preferred_element_type=jnp.float32)
    hidden = (jax.nn.gelu(gate, approximate=True) * upward).astype(jnp.bfloat16)
    summed = lax.psum_scatter(
        lax.dot_general(
            hidden, down_full, (((1,), (1,)), ((), ())), preferred_element_type=jnp.float32
        ).astype(jnp.bfloat16),
        "mlp",
        scatter_dimension=0,
        tiled=True,
    ).astype(jnp.float32)
    return (resid.astype(jnp.float32) + summed).astype(jnp.bfloat16)


def solution(mesh):
    return jax.shard_map(
        body,
        mesh=mesh,
        in_specs=(
            P(("req", "mlp"), None),
            P(),
            P(),
            P(),
            P(),
            P(),
            P("req", "mlp"),
            P("req", "mlp"),
            P("req", "mlp"),
            P(None, "req", None, None),
            P("req", None, None),
            P(),
            P(),
            P(),
        ),
        out_specs=P(("req", "mlp"), None),
        check_vma=False,
    )
```

profile of v0, /device:TPU:1, one launch (start us, length us, event | category | flops | bytes accessed | tf_op | source)
XLA Modules:
  0.0 438.2 jit_solution(3613787128685627271)
XLA Ops:
  13.8 1.7 fusion.35
  16.1 1.5 constant_dynamic-slice_fusion
  21.9 7.2 %convert_bitcast_fusion = bf16[16,2,512,256]{3,0,2,1:T(8,128)(2,1)} fusion(bf16[2,8,512,256]{3,2,1,0:T(8,128)(2,1)} %param.23, s32[16,2]{0,1:T(2,128)S(1)} %get-tuple-element.24, pred[16,2]{0,1:T(4,128)(4,1)S(1)} %fusion.54), kind=kOutput, calls=%fused_computation.15 | convolution fusion | flops 71303680 | bytes 12583072 | tf_op jit(solution)/shard_map/rln,lnsc->rlsc/dot_general | solution.py:113
  29.1 9.6 %copy.33 = bf16[16,2,512,256]{3,2,1,0:T(8,128)(2,1)} copy(bf16[16,2,512,256]{3,0,2,1:T(8,128)(2,1)} %convert_bitcast_fusion) | data formatting | bytes 16777216 | tf_op jit(solution)/shard_map/convert_element_type | solution.py:115
  38.8 8.9 %all-to-all-start = ((bf16[16,2,512,256]{3,2,1,0:T(8,128)(2,1)}), bf16[16,2,512,256]{3,2,1,0:T(8,128)(2,1)}, u32[]{:S(2)}, u32[]{:S(2)}) async-start(bf16[16,2,512,256]{3,2,1,0:T(8,128)(2,1)} %copy.33), calls=%async_computation | async-start | bytes 16777216 | tf_op jit(solution)/shard_map/all_to_all | solution.py:116
  48.8 4.3 fusion.37
  53.8 1.6 copy.44
  58.8 1.9 multiply_subtract_fusion
  62.3 11.8 %select_reduce_fusion = (f32[256,12]{0,1:T(8,128)S(1)}, f32[256,12,2048]{2,0,1:T(8,128)}) fusion(pred[256,2048]{1,0:T(8,128)(4,1)S(1)} %fusion.24, bf16[256,12,128]{2,0,1:T(8,128)(2,1)S(1)} %fusion.28, bf16[2048,256]{0,1:T(8,128)(2,1)} %all-gather.6.cloned.1.call-done), kind=kOutput, calls=%fused_computation.2 | convolution fusion | flops 1623192576 | bytes 27013120 | tf_op jit(solution)/shard_map/thd,kd->thk/dot_general | solution.py:29
  74.2 11.3 %fusion = f32[256,12]{0,1:T(8,128)S(1)} fusion(f32[256,12,2048]{2,0,1:T(8,128)} %get-tuple-element.27, f32[256,12]{0,1:T(8,128)S(1)} %get-tuple-element.18, pred[256,2048]{1,0:T(8,128)(4,1)S(1)} %fusion.24), kind=kLoop, calls=%fused_computation.3 | loop fusion | flops 18871296 | bytes 25714688 | tf_op jit(solution)/shard_map/reduce_sum | solution.py:41
  85.5 11.8 %fusion.4 = f32[256,12,128]{0,2,1:T(8,128)} fusion(f32[256,12,2048]{2,0,1:T(8,128)} %get-tuple-element.27, f32[256,12]{0,1:T(8,128)S(1)} %get-tuple-element.18, pred[256,2048]{1,0:T(8,128)(4,1)S(1)} %fusion.24, bf16[2048,256]{0,1:T(8,128)(2,1)S(1)} %copy-done.5), kind=kOutput, calls=%fused_computation.9 | convolution fusion | flops 1629487104 | bytes 27803648 | tf_op jit(solution)/shard_map/thk,kd->thd/dot_general | solution.py:35
  97.3 97.6 %all-to-all-done = bf16[16,2,512,256]{3,2,1,0:T(8,128)(2,1)} async-done(((bf16[16,2,512,256]{3,2,1,0:T(8,128)(2,1)}), bf16[16,2,512,256]{3,2,1,0:T(8,128)(2,1)}, u32[]{:S(2)}, u32[]{:S(2)}) %all-to-all-start) | async-done | bytes 8388640 | tf_op jit(solution)/shard_map/all_to_all | solution.py:116
  194.9 8.3 %fusion.10 = bf16[2,1,512,256]{3,1,2,0:T(2,128)(2,1)S(1)} fusion(pred[16,2,1,1]{0,2,3,1:T(4,128)(4,1)S(1)} %copy.38, bf16[16,2,512,256]{3,2,1,0:T(8,128)(2,1)} %all-to-all-done), kind=kOutput, calls=%fused_computation.13 | convolution fusion | flops 8388608 | bytes 8912928 | tf_op jit(solution)/shard_map/rl,rlsc->lsc/dot_general | solution.py:117
  203.4 8.0 %select_reduce_fusion.1 = (f32[256,12]{0,1:T(8,128)S(1)}, f32[256,12,1536]{2,0,1:T(8,128)}) fusion(pred[256,1536]{1,0:T(8,128)(4,1)S(1)} %fusion.30, bf16[256,12,128]{2,0,1:T(8,128)(2,1)S(1)} %fusion.28, bf16[1536,256]{1,0:T(8,128)(2,1)S(1)} %pad_maximum_fusion), kind=kOutput, calls=%fused_computation.6 | convolution fusion | flops 1217393664 | bytes 20459520 | tf_op jit(solution)/shard_map/thd,kd->thk/dot_general | solution.py:29
  211.5 10.5 %fusion.2 = f32[256,12]{0,1:T(8,128)S(1)} fusion(f32[256,12,1536]{2,0,1:T(8,128)} %get-tuple-element.29, f32[256,12]{0,1:T(8,128)S(1)} %is-finite_select_fusion, pred[256,1536]{1,0:T(8,128)(4,1)S(1)} %fusion.30), kind=kLoop, calls=%fused_computation.7 | loop fusion | flops 14152704 | bytes 19292160 | tf_op jit(solution)/shard_map/reduce_sum | solution.py:41
  222.0 8.7 %divide_convert_fusion = bf16[256,12,128]{0,2,1:T(8,128)(2,1)S(1)} fusion(f32[256,12,128]{0,2,1:T(8,128)} %fusion.4, f32[256,12,1536]{2,0,1:T(8,128)} %get-tuple-element.29, f32[256,12]{0,1:T(8,128)S(1)} %is-finite_select_fusion, pred[256,1536]{1,0:T(8,128)(4,1)S(1)} %fusion.30, f32[256,12]{0,1:T(8,128)S(1)} %get-tuple-element.5, ...), kind=kOutput, calls=%fused_computation.46 | convolution fusion | flops 1224867840 | bytes 22118400 | tf_op jit(solution)/shard_map/thk,kd->thd/dot_general | solution.py:35
  230.8 1.5 multiply_reduce_fusion
  234.7 44.8 %all-gather.8.cloned.1.call-done = bf16[2048,1536]{1,0:T(8,128)(2,1)} async-done(((bf16[256,1536]{1,0:T(8,128)(2,1)}), bf16[2048,1536]{1,0:T(8,128)(2,1)}) %all-gather.8.cloned.1.call-update) | async-done | bytes 6291472 | tf_op jit(solution)/shard_map/all_gather | solution.py:129
  279.4 9.3 %fusion.63 = f32[2048,576]{0,1:T(8,128)} fusion(bf16[2048,1536]{1,0:T(8,128)(2,1)} %all-gather.8.cloned.1.call-done, bf16[1536,576]{1,0:T(8,128)(2,1)} %all-gather.10.cloned.1.call-done), kind=kOutput, calls=%fused_computation.133 | convolution fusion | flops 3623878656 | bytes 12779520 | tf_op jit(solution)/shard_map/dot_general | solution.py:135
  288.8 36.4 %all-gather.14.cloned.1.call-done = bf16[1536,576]{1,0:T(8,128)(2,1)} async-done(((bf16[96,576]{1,0:T(8,128)(2,1)}), bf16[1536,576]{1,0:T(8,128)(2,1)}) %all-gather.14.cloned.1.call-update) | async-done | bytes 1769488 | tf_op jit(solution)/shard_map/all_gather | solution.py:133
  325.2 46.1 %all-gather.12.cloned.1.call-done = bf16[1536,576]{1,0:T(8,128)(2,1)} async-done(((bf16[96,576]{1,0:T(8,128)(2,1)}), bf16[1536,576]{1,0:T(8,128)(2,1)}) %all-gather.12.cloned.1.call-update) | async-done | bytes 1769488 | tf_op jit(solution)/shard_map/all_gather | solution.py:132
  371.2 15.6 %convolution_convert_fusion = bf16[2048,1536]{1,0:T(8,128)(2,1)} fusion(bf16[1536,576]{1,0:T(8,128)(2,1)} %all-gather.14.cloned.1.call-done, f32[2048,576]{0,1:T(8,128)} %fusion.63, bf16[2048,1536]{1,0:T(8,128)(2,1)} %all-gather.8.cloned.1.call-done, bf16[1536,576]{1,0:T(8,128)(2,1)} %all-gather.12.cloned.1.call-done), kind=kOutput, calls=%fused_computation.16 | convolution fusion | flops 7262699520 | bytes 20840448 | tf_op jit(solution)/shard_map/dot_general | solution.py:139
  386.8 42.0 %reduce-scatter.2.cloned.1.call-done = bf16[256,1536]{1,0:T(8,128)(2,1)} async-done(((bf16[2048,1536]{1,0:T(8,128)(2,1)}), bf16[256,1536]{1,0:T(8,128)(2,1)}) %reduce-scatter.2.cloned.1.call-update) | async-done | bytes 786448 | tf_op jit(solution)/shard_map/reduce_scatter | solution.py:138
  428.9 2.2 add_convert_fusion
  (80 shorter events, 15.6 us)
Async XLA Ops:
  6.5 7.2 %copy-start = (bf16[1536,256]{1,0:T(8,128)(2,1)S(1)}, bf16[1536,256]{1,0:T(8,128)(2,1)}, u32[]{:S(2)}) copy-start(bf16[1536,256]{1,0:T(8,128)(2,1)} %param.17) | copy-start | bytes 2359300
  6.5 15.3 %copy-start.8 = (s32[16]{0:T(128)S(1)}, s32[16]{0:T(128)}, u32[]{:S(2)}) copy-start(s32[16]{0:T(128)} %param.25) | copy-start | bytes 196
  6.5 14.7 %copy-start.2 = (s32[128]{0:T(128)S(1)}, s32[128]{0:T(128)}, u32[]{:S(2)}) copy-start(s32[128]{0:T(128)} %param.26) | copy-start | bytes 1540
  6.5 55.8 %all-gather.6.cloned.1.call-start = ((), (), s32[]{:S(2)}) async-start(), calls=%async_computation.2 | async-start | bytes 1179648 | tf_op jit(solution)/shard_map/all_gather | solution.py:97
  38.8 10.0 %copy-start.3 = (bf16[256,1536]{1,0:T(8,128)(2,1)S(1)}, bf16[256,1536]{1,0:T(8,128)(2,1)}, u32[]{:S(2)}) copy-start(bf16[256,1536]{1,0:T(8,128)(2,1)} %param.14) | copy-start | bytes 2359300
  38.8 10.0 %copy-start.9 = (f32[1536]{0:T(1024)S(1)}, f32[1536]{0:T(1024)}, u32[]{:S(2)}) copy-start(f32[1536]{0:T(1024)} %param.15) | copy-start | bytes 18436
  38.8 156.1 %all-to-all-start = ((bf16[16,2,512,256]{3,2,1,0:T(8,128)(2,1)}), bf16[16,2,512,256]{3,2,1,0:T(8,128)(2,1)}, u32[]{:S(2)}, u32[]{:S(2)}) async-start(bf16[16,2,512,256]{3,2,1,0:T(8,128)(2,1)} %copy.33), calls=%async_computation | async-start | bytes 16777216 | tf_op jit(solution)/shard_map/all_to_all | solution.py:116
  47.7 187.0 %all-gather.10.cloned.1.call-start = ((), (), s32[]{:S(2)}) async-start(), calls=%async_computation.4 | async-start | bytes 2088960 | tf_op jit(solution)/shard_map/all_gather | solution.py:131
  48.4 231.0 %all-gather.8.cloned.1.call-start = ((), (), s32[]{:S(2)}) async-start(), calls=%async_computation.3 | async-start | bytes 7077888 | tf_op jit(solution)/shard_map/all_gather | solution.py:129
  74.2 11.4 %copy-start.5 = (bf16[2048,256]{0,1:T(8,128)(2,1)S(1)}, bf16[2048,256]{0,1:T(8,128)(2,1)}, u32[]{:S(2)}) copy-start(bf16[2048,256]{0,1:T(8,128)(2,1)} %all-gather.6.cloned.1.call-done) | copy-start | bytes 3145732
  97.3 106.0 %copy-start.6 = (bf16[1,512,256]{2,1,0:T(8,128)(2,1)S(1)}, bf16[1,512,256]{2,1,0:T(8,128)(2,1)}, u32[]{:S(2)}) copy-start(bf16[1,512,256]{2,1,0:T(8,128)(2,1)} %param.24) | copy-start | bytes 786436
  211.5 19.3 %slice-start = ((s8[4718592]{0:T(1024)(128)(4,1)}), s8[524288]{0:T(1024)(128)(4,1)S(1)}, s32[]{:S(2)}) async-start(s8[4718592]{0:T(1024)(128)(4,1)} %bitcast.58), calls=%async_computation.8 | async-start | bytes 1048576
  222.0 8.8 %slice-start.1 = ((s8[4718592]{0:T(1024)(128)(4,1)}), s8[4194304]{0:T(1024)(128)(4,1)S(1)}, s32[]{:S(2)}) async-start(s8[4718592]{0:T(1024)(128)(4,1)} %bitcast.58), calls=%async_computation.9 | async-start | bytes 8388608
  222.0 8.8 %copy-start.4 = (bf16[256,1536]{1,0:T(8,128)(2,1)S(1)}, bf16[256,1536]{1,0:T(8,128)(2,1)}, u32[]{:S(2)}) copy-start(bf16[256,1536]{1,0:T(8,128)(2,1)} %param.14) | copy-start | bytes 2359300
  230.8 1.5 copy-start.7
  233.4 91.7 %all-gather.14.cloned.1.call-start = ((), (), s32[]{:S(2)}) async-start(), calls=%async_computation.6 | async-start | bytes 2088960 | tf_op jit(solution)/shard_map/all_gather | solution.py:133
  234.0 137.2 %all-gather.12.cloned.1.call-start = ((), (), s32[]{:S(2)}) async-start(), calls=%async_computation.5 | async-start | bytes 2088960 | tf_op jit(solution)/shard_map/all_gather | solution.py:132
  234.6 194.3 %reduce-scatter.2.cloned.1.call-start = ((), (), s32[]{:S(2)}) async-start(), calls=%async_computation.7 | async-start | bytes 7077888 | tf_op jit(solution)/shard_map/reduce_scatter | solution.py:138
  386.8 44.3 %copy-start.1 = (bf16[1536,256]{1,0:T(8,128)(2,1)S(1)}, bf16[1536,256]{1,0:T(8,128)(2,1)}, u32[]{:S(2)}) copy-start(bf16[1536,256]{1,0:T(8,128)(2,1)} %param.17) | copy-start | bytes 2359300
Sparse Core Ops, SparseCore 0:
  20.7 26.9 all-gather.5
  50.7 139.0 all-gather.9
  233.6 45.8 all-gather.7
  281.5 43.6 all-gather.13
  327.2 43.9 all-gather.11
  387.0 41.8 reduce-scatter.1
where the time goes:
time: 444 us; the launch traced here: 438 us
  waiting for transfers between devices  269 us (61%)
  matrix products  88.4 us (20%)
  other arithmetic  35 us (8%)
  between operations  19.9 us (4%)
  local copies, waits for them, and re-layouts  16.9 us (4%)
  starting transfers between devices  9.38 us (2%)
    all_to_all x1, waiting for transfers between devices, body(): lax.all_to_all(outgoing, 'req', split_axis=0, concat_axis=0, tiled=True)  97.6 us
    all_gather x1, waiting for transfers between devices, body(): lax.all_gather(w_up, 'req', axis=0, tiled=True)  46.1 us
    all_gather x1, waiting for transfers between devices, body(): all_rows = lax.all_gather(ffn_in, 'mlp', axis=0, tiled=True)  44.8 us
    reduce_scatter x1, waiting for transfers between devices, body(): lax.psum_scatter(lax.dot_general(hidden, down_full, (((1,), (1,)), ((), (...  42 us
    all_gather x1, waiting for transfers between devices, body(): lax.all_gather(w_down, 'req', axis=0, tiled=True)  36.4 us
    reduce_sum x2, other arithmetic, attend(): return (top, jnp.sum(weights, axis=-1), mixed)  21.8 us
    dot_general x2, matrix products, attend(): jnp.einsum('thk,kd->thd', weights.astype(jnp.bfloat16), piece[:, HD:], pr...  20.5 us
    dot_general x2, matrix products, attend(): jnp.einsum('thd,kd->thk', queries, piece[:, :HD], preferred_element_type=...  19.9 us
  transfers between devices with their start and end apart: 7, of which 5 were waited for; matrix products, arithmetic and copies ran while one was open for 26% of the time, Pallas kernels for 0%

commit v1 on v0

--- a/solution.py
+++ b/solution.py
@@ -7,6 +7,28 @@
 HD = 128
 WINDOW = 1024
 EPS = 1e-06
+
+
+def laid_out(blocks, dim):
+    shape = list(blocks.shape[1:])
+    shape[dim] *= blocks.shape[0]
+    return jnp.moveaxis(blocks, 0, dim).reshape(shape)
+
+
+def ring_gather(shard, axis, dim):
+    devices = lax.axis_size(axis)
+    pairs = [(i, (i + 1) % devices) for i in range(devices)]
+    back = [(b, a) for a, b in pairs]
+    lower, upper = ([], [])
+    for step in range(devices - 1):
+        if step % 2 == 0:
+            lower.append(lax.ppermute(lower[-1] if lower else shard, axis, pairs))
+        else:
+            upper.append(lax.ppermute(upper[-1] if upper else shard, axis, back))
+    parts = jnp.stack([*lower[::-1], shard, *upper])
+    shift = lax.axis_index(axis) - len(lower)
+    parts = parts[(jnp.arange(devices) - shift) % devices]
+    return laid_out(parts, dim)
 
 
 def rms_scale(values, gain):
@@ -130,7 +152,7 @@
     gate_full, up_full, down_full = (
         lax.all_gather(w_gate, "req", axis=0, tiled=True),
         lax.all_gather(w_up, "req", axis=0, tiled=True),
-        lax.all_gather(w_down, "req", axis=0, tiled=True),
+        ring_gather(w_down, "req", 0),
     )
     gate = jnp.dot(all_rows, gate_full, preferred_element_type=jnp.float32)
     upward = jnp.dot(all_rows, up_full, preferred_element_type=jnp.float32)

time: 444 us -> 397 us (0.89)
  waiting for transfers between devices: 269 us -> 174 us
  starting transfers between devices: 9.38 us -> 43.9 us
  local copies, waits for them, and re-layouts: 16.9 us -> 31.1 us
    all_gather x1, waiting for transfers between devices: 44.8 us -> 0.01 us  [body(): all_rows = lax.all_gather(ffn_in, 'mlp', axis=0, tiled=True)]
    all_gather x1, waiting for transfers between devices: 46.1 us -> 9.49 us  [body(): lax.all_gather(w_up, 'req', axis=0, tiled=True)]
    all_gather x1 -> x0, waiting for transfers between devices: 36.4 us -> none  [body(): lax.all_gather(w_down, 'req', axis=0, tiled=True)]
    ppermute x0 -> x15, starting transfers between devices: none -> 34.6 us  [the longest x7 34.5 us: ring_gather(): upper.append(lax.ppermute(upper[-1] if upper else shard, axis, back))]
    ppermute x0 -> x15, waiting for transfers between devices: none -> 23.4 us  [the longest x8 23.4 us: ring_gather(): lower.append(lax.ppermute(lower[-1] if lower else shard, axis, pairs))]
    unnamed x26 -> x45, local copies, waits for them, and re-layouts: 2.16 us -> 12.9 us
  transfers between devices with their start and end apart: 7 -> 21, of which waited for: 5 -> 11; matrix products, arithmetic and copies ran while one was open for 26% -> 33% of each run, Pallas kernels for 0% -> 0%
where the time goes in v1:
time: 397 us; the launch traced here: 391 us
  waiting for transfers between devices  174 us (44%)
  matrix products  88.2 us (22%)
  starting transfers between devices  43.9 us (11%)
  other arithmetic  34.4 us (9%)
  local copies, waits for them, and re-layouts  31.1 us (8%)
  between operations  19.7 us (5%)
    all_to_all x1, waiting for transfers between devices, body(): lax.all_to_all(outgoing, 'req', split_axis=0, concat_axis=0, tiled=True)  98.3 us
    reduce_scatter x1, waiting for transfers between devices, body(): lax.psum_scatter(lax.dot_general(hidden, down_full, (((1,), (1,)), ((), (...  42 us
    ppermute x7, starting transfers between devices, ring_gather(): upper.append(lax.ppermute(upper[-1] if upper else shard, axis, back))  34.5 us
    ppermute x8, waiting for transfers between devices, ring_gather(): lower.append(lax.ppermute(lower[-1] if lower else shard, axis, pairs))  23.4 us
    reduce_sum x2, other arithmetic, attend(): return (top, jnp.sum(weights, axis=-1), mixed)  21.8 us
    dot_general x2, matrix products, attend(): jnp.einsum('thk,kd->thd', weights.astype(jnp.bfloat16), piece[:, HD:], pr...  20.5 us
    dot_general x2, matrix products, attend(): jnp.einsum('thd,kd->thk', queries, piece[:, :HD], preferred_element_type=...  19.9 us
    dot_general x1, matrix products, body(): lax.dot_general(hidden, down_full, (((1,), (1,)), ((), ())), preferred_el...  15.4 us
  transfers between devices with their start and end apart: 21, of which 11 were waited for; matrix products, arithmetic and copies ran while one was open for 33% of the time, Pallas kernels for 0%

profile of v1, /device:TPU:1, one launch (start us, length us, event | category | flops | bytes accessed | tf_op | source)
XLA Modules:
  0.0 391.5 jit_solution(16163174754400368248)
XLA Ops:
  20.5 7.2 %convert_bitcast_fusion = bf16[16,2,512,256]{3,0,2,1:T(8,128)(2,1)} fusion(bf16[2,8,512,256]{3,2,1,0:T(8,128)(2,1)} %param.23, s32[16,2]{0,1:T(2,128)S(1)} %get-tuple-element.24, pred[16,2]{0,1:T(4,128)(4,1)S(1)} %fusion.54), kind=kOutput, calls=%fused_computation.16 | convolution fusion | flops 71303680 | bytes 12583072 | tf_op jit(solution)/shard_map/rln,lnsc->rlsc/dot_general | solution.py:135
  27.8 9.6 %copy.33 = bf16[16,2,512,256]{3,2,1,0:T(8,128)(2,1)} copy(bf16[16,2,512,256]{3,0,2,1:T(8,128)(2,1)} %convert_bitcast_fusion) | data formatting | bytes 16777216 | tf_op jit(solution)/shard_map/convert_element_type | solution.py:137
  37.4 8.9 %all-to-all-start = ((bf16[16,2,512,256]{3,2,1,0:T(8,128)(2,1)}), bf16[16,2,512,256]{3,2,1,0:T(8,128)(2,1)}, u32[]{:S(2)}, u32[]{:S(2)}) async-start(bf16[16,2,512,256]{3,2,1,0:T(8,128)(2,1)} %copy.33), calls=%async_computation | async-start | bytes 16777216 | tf_op jit(solution)/shard_map/all_to_all | solution.py:138
  47.4 4.3 %fusion.37 = f32[256,1536]{0,1:T(8,128)S(1)} fusion(bf16[1536,1536]{1,0:T(8,128)(2,1)} %param.16, bf16[256,1536]{1,0:T(8,128)(2,1)S(1)} %copy-done.3, f32[1536]{0:T(1024)S(1)} %copy-done.11, f32[256]{0:T(256)S(1)} %add_rsqrt_fusion.1), kind=kOutput, calls=%fused_computation.63 | convolution fusion | flops 1209532416 | bytes 7085056 | tf_op jit(solution)/shard_map/dot_general | solution.py:106
  61.0 11.8 %select_reduce_fusion = (f32[256,12]{0,1:T(8,128)S(1)}, f32[256,12,2048]{2,0,1:T(8,128)}) fusion(pred[256,2048]{1,0:T(8,128)(4,1)S(1)} %fusion.24, bf16[256,12,128]{2,0,1:T(8,128)(2,1)S(1)} %fusion.28, bf16[2048,256]{0,1:T(8,128)(2,1)} %all-gather.5.cloned.1.call-done), kind=kOutput, calls=%fused_computation.3 | convolution fusion | flops 1623192576 | bytes 27013120 | tf_op jit(solution)/shard_map/thd,kd->thk/dot_general | solution.py:51
  72.9 11.3 %fusion = f32[256,12]{0,1:T(8,128)S(1)} fusion(f32[256,12,2048]{2,0,1:T(8,128)} %get-tuple-element.27, f32[256,12]{0,1:T(8,128)S(1)} %get-tuple-element.18, pred[256,2048]{1,0:T(8,128)(4,1)S(1)} %fusion.24), kind=kLoop, calls=%fused_computation.4 | loop fusion | flops 18871296 | bytes 25714688 | tf_op jit(solution)/shard_map/reduce_sum | solution.py:63
  84.2 11.8 %fusion.4 = f32[256,12,128]{0,2,1:T(8,128)} fusion(f32[256,12,2048]{2,0,1:T(8,128)} %get-tuple-element.27, f32[256,12]{0,1:T(8,128)S(1)} %get-tuple-element.18, pred[256,2048]{1,0:T(8,128)(4,1)S(1)} %fusion.24, bf16[2048,256]{0,1:T(8,128)(2,1)S(1)} %copy-done.5), kind=kOutput, calls=%fused_computation.10 | convolution fusion | flops 1629487104 | bytes 27803648 | tf_op jit(solution)/shard_map/thk,kd->thd/dot_general | solution.py:57
  96.0 98.3 %all-to-all-done = bf16[16,2,512,256]{3,2,1,0:T(8,128)(2,1)} async-done(((bf16[16,2,512,256]{3,2,1,0:T(8,128)(2,1)}), bf16[16,2,512,256]{3,2,1,0:T(8,128)(2,1)}, u32[]{:S(2)}, u32[]{:S(2)}) %all-to-all-start) | async-done | bytes 8388640 | tf_op jit(solution)/shard_map/all_to_all | solution.py:138
  194.3 8.3 %fusion.10 = bf16[2,1,512,256]{3,1,2,0:T(2,128)(2,1)S(1)} fusion(pred[16,2,1,1]{0,2,3,1:T(4,128)(4,1)S(1)} %copy.38, bf16[16,2,512,256]{3,2,1,0:T(8,128)(2,1)} %all-to-all-done), kind=kOutput, calls=%fused_computation.14 | convolution fusion | flops 8388608 | bytes 8912928 | tf_op jit(solution)/shard_map/rl,rlsc->lsc/dot_general | solution.py:139
  203.6 8.1 %select_reduce_fusion.1 = (f32[256,12]{0,1:T(8,128)S(1)}, f32[256,12,1536]{2,0,1:T(8,128)}) fusion(pred[256,1536]{1,0:T(8,128)(4,1)S(1)} %fusion.30, bf16[256,12,128]{2,0,1:T(8,128)(2,1)S(1)} %fusion.28, bf16[1536,256]{1,0:T(8,128)(2,1)S(1)} %pad_maximum_fusion), kind=kOutput, calls=%fused_computation.7 | convolution fusion | flops 1217393664 | bytes 20459520 | tf_op jit(solution)/shard_map/thd,kd->thk/dot_general | solution.py:51
  211.7 10.5 %fusion.2 = f32[256,12]{0,1:T(8,128)S(1)} fusion(f32[256,12,1536]{2,0,1:T(8,128)} %get-tuple-element.29, f32[256,12]{0,1:T(8,128)S(1)} %is-finite_select_fusion, pred[256,1536]{1,0:T(8,128)(4,1)S(1)} %fusion.30), kind=kLoop, calls=%fused_computation.8 | loop fusion | flops 14152704 | bytes 19292160 | tf_op jit(solution)/shard_map/reduce_sum | solution.py:63
  222.3 8.7 %divide_convert_fusion = bf16[256,12,128]{0,2,1:T(8,128)(2,1)S(1)} fusion(f32[256,12,128]{0,2,1:T(8,128)} %fusion.4, f32[256,12,1536]{2,0,1:T(8,128)} %get-tuple-element.29, f32[256,12]{0,1:T(8,128)S(1)} %is-finite_select_fusion, pred[256,1536]{1,0:T(8,128)(4,1)S(1)} %fusion.30, f32[256,12]{0,1:T(8,128)S(1)} %get-tuple-element.5, ...), kind=kOutput, calls=%fused_computation.47 | convolution fusion | flops 1224867840 | bytes 22118400 | tf_op jit(solution)/shard_map/thk,kd->thd/dot_general | solution.py:57
  233.9 7.0 %collective-permute-done = bf16[96,576]{1,0:T(8,128)(2,1)S(1)} collective-permute-done((bf16[96,576]{1,0:T(8,128)(2,1)S(1)}, bf16[96,576]{1,0:T(8,128)(2,1)S(1)}, u32[]{:S(2)}, u32[]{:S(2)}) %collective-permute-start) | collective-permute-done | bytes 110624 | tf_op jit(solution)/shard_map/ppermute | solution.py:25
  240.9 4.8 %collective-permute-start.8 = (bf16[96,576]{1,0:T(8,128)(2,1)S(1)}, bf16[96,576]{1,0:T(8,128)(2,1)S(1)}, u32[]{:S(2)}, u32[]{:S(2)}) collective-permute-start(bf16[96,576]{1,0:T(8,128)(2,1)S(1)} %copy-done.7), channel_id=1, source_target_pairs={{8,0},{16,8},{24,16},{32,24},{40,32},{48,40},{56,48},{64,56},{72,6... | collective-permute-start | bytes 331784 | tf_op jit(solution)/shard_map/ppermute | solution.py:27
  248.0 4.8 %collective-permute-start.9 = (bf16[96,576]{1,0:T(8,128)(2,1)S(1)}, bf16[96,576]{1,0:T(8,128)(2,1)S(1)}, u32[]{:S(2)}, u32[]{:S(2)}) collective-permute-start(bf16[96,576]{1,0:T(8,128)(2,1)S(1)} %collective-permute-done.8), channel_id=1, source_target_pairs={{8,0},{16,8},{24,16},{32,24},{40,32},{48,40},{56,48},{64,56},{72,6... | collective-permute-start | bytes 331784 | tf_op jit(solution)/shard_map/ppermute | solution.py:27
  255.0 4.8 %collective-permute-start.10 = (bf16[96,576]{1,0:T(8,128)(2,1)S(1)}, bf16[96,576]{1,0:T(8,128)(2,1)S(1)}, u32[]{:S(2)}, u32[]{:S(2)}) collective-permute-start(bf16[96,576]{1,0:T(8,128)(2,1)S(1)} %collective-permute-done.9), channel_id=1, source_target_pairs={{8,0},{16,8},{24,16},{32,24},{40,32},{48,40},{56,48},{64,56},{72,6... | collective-permute-start | bytes 331784 | tf_op jit(solution)/shard_map/ppermute | solution.py:27
  262.1 4.8 %collective-permute-start.11 = (bf16[96,576]{1,0:T(8,128)(2,1)S(1)}, bf16[96,576]{1,0:T(8,128)(2,1)S(1)}, u32[]{:S(2)}, u32[]{:S(2)}) collective-permute-start(bf16[96,576]{1,0:T(8,128)(2,1)S(1)} %collective-permute-done.10), channel_id=1, source_target_pairs={{8,0},{16,8},{24,16},{32,24},{40,32},{48,40},{56,48},{64,56},{72,6... | collective-permute-start | bytes 331784 | tf_op jit(solution)/shard_map/ppermute | solution.py:27
  269.2 4.9 %collective-permute-start.12 = (bf16[96,576]{1,0:T(8,128)(2,1)S(1)}, bf16[96,576]{1,0:T(8,128)(2,1)S(1)}, u32[]{:S(2)}, u32[]{:S(2)}) collective-permute-start(bf16[96,576]{1,0:T(8,128)(2,1)S(1)} %collective-permute-done.11), channel_id=1, source_target_pairs={{8,0},{16,8},{24,16},{32,24},{40,32},{48,40},{56,48},{64,56},{72,6... | collective-permute-start | bytes 331784 | tf_op jit(solution)/shard_map/ppermute | solution.py:27
  277.1 5.2 %collective-permute-start.13 = (bf16[96,576]{1,0:T(8,128)(2,1)S(1)}, bf16[96,576]{1,0:T(8,128)(2,1)S(1)}, u32[]{:S(2)}, u32[]{:S(2)}) collective-permute-start(bf16[96,576]{1,0:T(8,128)(2,1)S(1)} %collective-permute-done.12), channel_id=1, source_target_pairs={{8,0},{16,8},{24,16},{32,24},{40,32},{48,40},{56,48},{64,56},{72,6... | collective-permute-start | bytes 331784 | tf_op jit(solution)/shard_map/ppermute | solution.py:27
  285.0 5.3 %collective-permute-start.14 = (bf16[96,576]{1,0:T(8,128)(2,1)S(1)}, bf16[96,576]{1,0:T(8,128)(2,1)S(1)}, u32[]{:S(2)}, u32[]{:S(2)}) collective-permute-start(bf16[96,576]{1,0:T(8,128)(2,1)S(1)} %collective-permute-done.13), channel_id=1, source_target_pairs={{8,0},{16,8},{24,16},{32,24},{40,32},{48,40},{56,48},{64,56},{72,6... | collective-permute-start | bytes 331784 | tf_op jit(solution)/shard_map/ppermute | solution.py:27
  306.2 9.3 %fusion.65 = f32[2048,576]{0,1:T(8,128)} fusion(bf16[2048,1536]{1,0:T(8,128)(2,1)} %all-gather.7.cloned.1.call-done, bf16[1536,576]{1,0:T(8,128)(2,1)} %all-gather.9.cloned.1.call-done), kind=kOutput, calls=%fused_computation.157 | convolution fusion | flops 3623878656 | bytes 12779520 | tf_op jit(solution)/shard_map/dot_general | solution.py:157
  315.5 9.5 %all-gather.11.cloned.1.call-done = bf16[1536,576]{1,0:T(8,128)(2,1)} async-done(((bf16[96,576]{1,0:T(8,128)(2,1)}), bf16[1536,576]{1,0:T(8,128)(2,1)}) %all-gather.11.cloned.1.call-update) | async-done | bytes 1769488 | tf_op jit(solution)/shard_map/all_gather | solution.py:154
  325.0 15.4 %convolution_convert_fusion = bf16[2048,1536]{1,0:T(8,128)(2,1)} fusion(bf16[1536,576]{1,0:T(8,128)(2,1)} %bitcast.97, f32[2048,576]{0,1:T(8,128)} %fusion.65, bf16[2048,1536]{1,0:T(8,128)(2,1)} %all-gather.7.cloned.1.call-done, bf16[1536,576]{1,0:T(8,128)(2,1)} %all-gather.11.cloned.1.call-done), kind=kOutput, calls=%fused_computation.17 | convolution fusion | flops 7262699520 | bytes 20840448 | tf_op jit(solution)/shard_map/dot_general | solution.py:161
  340.5 42.0 %reduce-scatter.2.cloned.1.call-done = bf16[256,1536]{1,0:T(8,128)(2,1)} async-done(((bf16[2048,1536]{1,0:T(8,128)(2,1)}), bf16[256,1536]{1,0:T(8,128)(2,1)}) %reduce-scatter.2.cloned.1.call-update) | async-done | bytes 786448 | tf_op jit(solution)/shard_map/reduce_scatter | solution.py:160
  (130 shorter events, 55.0 us)
Async XLA Ops:
  6.5 54.5 %all-gather.5.cloned.1.call-start = ((), (), s32[]{:S(2)}) async-start(), calls=%async_computation.2 | async-start | bytes 1179648 | tf_op jit(solution)/shard_map/all_gather | solution.py:119
  37.4 157.0 %all-to-all-start = ((bf16[16,2,512,256]{3,2,1,0:T(8,128)(2,1)}), bf16[16,2,512,256]{3,2,1,0:T(8,128)(2,1)}, u32[]{:S(2)}, u32[]{:S(2)}) async-start(bf16[16,2,512,256]{3,2,1,0:T(8,128)(2,1)} %copy.33), calls=%async_computation | async-start | bytes 16777216 | tf_op jit(solution)/shard_map/all_to_all | solution.py:138
  46.2 259.9 %all-gather.9.cloned.1.call-start = ((), (), s32[]{:S(2)}) async-start(), calls=%async_computation.4 | async-start | bytes 2088960 | tf_op jit(solution)/shard_map/all_gather | solution.py:153
  47.0 259.2 %all-gather.7.cloned.1.call-start = ((), (), s32[]{:S(2)}) async-start(), calls=%async_computation.3 | async-start | bytes 7077888 | tf_op jit(solution)/shard_map/all_gather | solution.py:151
  72.9 11.4 %copy-start.5 = (bf16[2048,256]{0,1:T(8,128)(2,1)S(1)}, bf16[2048,256]{0,1:T(8,128)(2,1)}, u32[]{:S(2)}) copy-start(bf16[2048,256]{0,1:T(8,128)(2,1)} %all-gather.5.cloned.1.call-done) | copy-start | bytes 3145732
  211.7 19.3 %slice-start = ((s8[4718592]{0:T(1024)(128)(4,1)}), s8[524288]{0:T(1024)(128)(4,1)S(1)}, s32[]{:S(2)}) async-start(s8[4718592]{0:T(1024)(128)(4,1)} %bitcast.93), calls=%async_computation.7 | async-start | bytes 1048576
  233.7 91.3 %all-gather.11.cloned.1.call-start = ((), (), s32[]{:S(2)}) async-start(), calls=%async_computation.5 | async-start | bytes 2088960 | tf_op jit(solution)/shard_map/all_gather | solution.py:154
  233.8 7.1 %collective-permute-start = (bf16[96,576]{1,0:T(8,128)(2,1)S(1)}, bf16[96,576]{1,0:T(8,128)(2,1)S(1)}, u32[]{:S(2)}, u32[]{:S(2)}) collective-permute-start(bf16[96,576]{1,0:T(8,128)(2,1)S(1)} %copy-done.7), channel_id=1, source_target_pairs={{0,8},{8,16},{16,24},{24,32},{32,40},{40,48},{48,56},{56,64},{64,7... | collective-permute-start | bytes 331784 | tf_op jit(solution)/shard_map/ppermute | solution.py:25
  240.9 7.1 %collective-permute-start.1 = (bf16[96,576]{1,0:T(8,128)(2,1)S(1)}, bf16[96,576]{1,0:T(8,128)(2,1)S(1)}, u32[]{:S(2)}, u32[]{:S(2)}) collective-permute-start(bf16[96,576]{1,0:T(8,128)(2,1)S(1)} %collective-permute-done), channel_id=1, source_target_pairs={{0,8},{8,16},{16,24},{24,32},{32,40},{40,48},{48,56},{56,64},{64,7... | collective-permute-start | bytes 331784 | tf_op jit(solution)/shard_map/ppermute | solution.py:25
  240.9 7.1 %collective-permute-start.8 = (bf16[96,576]{1,0:T(8,128)(2,1)S(1)}, bf16[96,576]{1,0:T(8,128)(2,1)S(1)}, u32[]{:S(2)}, u32[]{:S(2)}) collective-permute-start(bf16[96,576]{1,0:T(8,128)(2,1)S(1)} %copy-done.7), channel_id=1, source_target_pairs={{8,0},{16,8},{24,16},{32,24},{40,32},{48,40},{56,48},{64,56},{72,6... | collective-permute-start | bytes 331784 | tf_op jit(solution)/shard_map/ppermute | solution.py:27
  248.0 7.1 %collective-permute-start.2 = (bf16[96,576]{1,0:T(8,128)(2,1)S(1)}, bf16[96,576]{1,0:T(8,128)(2,1)S(1)}, u32[]{:S(2)}, u32[]{:S(2)}) collective-permute-start(bf16[96,576]{1,0:T(8,128)(2,1)S(1)} %collective-permute-done.1), channel_id=1, source_target_pairs={{0,8},{8,16},{16,24},{24,32},{32,40},{40,48},{48,56},{56,64},{64,7... | collective-permute-start | bytes 331784 | tf_op jit(solution)/shard_map/ppermute | solution.py:25
  248.0 7.1 %collective-permute-start.9 = (bf16[96,576]{1,0:T(8,128)(2,1)S(1)}, bf16[96,576]{1,0:T(8,128)(2,1)S(1)}, u32[]{:S(2)}, u32[]{:S(2)}) collective-permute-start(bf16[96,576]{1,0:T(8,128)(2,1)S(1)} %collective-permute-done.8), channel_id=1, source_target_pairs={{8,0},{16,8},{24,16},{32,24},{40,32},{48,40},{56,48},{64,56},{72,6... | collective-permute-start | bytes 331784 | tf_op jit(solution)/shard_map/ppermute | solution.py:27
  255.0 7.1 %collective-permute-start.3 = (bf16[96,576]{1,0:T(8,128)(2,1)S(1)}, bf16[96,576]{1,0:T(8,128)(2,1)S(1)}, u32[]{:S(2)}, u32[]{:S(2)}) collective-permute-start(bf16[96,576]{1,0:T(8,128)(2,1)S(1)} %collective-permute-done.2), channel_id=1, source_target_pairs={{0,8},{8,16},{16,24},{24,32},{32,40},{40,48},{48,56},{56,64},{64,7... | collective-permute-start | bytes 331784 | tf_op jit(solution)/shard_map/ppermute | solution.py:25
  255.0 7.1 %collective-permute-start.10 = (bf16[96,576]{1,0:T(8,128)(2,1)S(1)}, bf16[96,576]{1,0:T(8,128)(2,1)S(1)}, u32[]{:S(2)}, u32[]{:S(2)}) collective-permute-start(bf16[96,576]{1,0:T(8,128)(2,1)S(1)} %collective-permute-done.9), channel_id=1, source_target_pairs={{8,0},{16,8},{24,16},{32,24},{40,32},{48,40},{56,48},{64,56},{72,6... | collective-permute-start | bytes 331784 | tf_op jit(solution)/shard_map/ppermute | solution.py:27
  262.1 7.1 %collective-permute-start.4 = (bf16[96,576]{1,0:T(8,128)(2,1)S(1)}, bf16[96,576]{1,0:T(8,128)(2,1)S(1)}, u32[]{:S(2)}, u32[]{:S(2)}) collective-permute-start(bf16[96,576]{1,0:T(8,128)(2,1)S(1)} %collective-permute-done.3), channel_id=1, source_target_pairs={{0,8},{8,16},{16,24},{24,32},{32,40},{40,48},{48,56},{56,64},{64,7... | collective-permute-start | bytes 331784 | tf_op jit(solution)/shard_map/ppermute | solution.py:25
  262.1 7.1 %collective-permute-start.11 = (bf16[96,576]{1,0:T(8,128)(2,1)S(1)}, bf16[96,576]{1,0:T(8,128)(2,1)S(1)}, u32[]{:S(2)}, u32[]{:S(2)}) collective-permute-start(bf16[96,576]{1,0:T(8,128)(2,1)S(1)} %collective-permute-done.10), channel_id=1, source_target_pairs={{8,0},{16,8},{24,16},{32,24},{40,32},{48,40},{56,48},{64,56},{72,6... | collective-permute-start | bytes 331784 | tf_op jit(solution)/shard_map/ppermute | solution.py:27
  269.1 8.0 %collective-permute-start.5 = (bf16[96,576]{1,0:T(8,128)(2,1)S(1)}, bf16[96,576]{1,0:T(8,128)(2,1)S(1)}, u32[]{:S(2)}, u32[]{:S(2)}) collective-permute-start(bf16[96,576]{1,0:T(8,128)(2,1)S(1)} %collective-permute-done.4), channel_id=1, source_target_pairs={{0,8},{8,16},{16,24},{24,32},{32,40},{40,48},{48,56},{56,64},{64,7... | collective-permute-start | bytes 331784 | tf_op jit(solution)/shard_map/ppermute | solution.py:25
  269.1 113.4 %reduce-scatter.2.cloned.1.call-start = ((), (), s32[]{:S(2)}) async-start(), calls=%async_computation.6 | async-start | bytes 7077888 | tf_op jit(solution)/shard_map/reduce_scatter | solution.py:160
  269.2 7.9 %collective-permute-start.12 = (bf16[96,576]{1,0:T(8,128)(2,1)S(1)}, bf16[96,576]{1,0:T(8,128)(2,1)S(1)}, u32[]{:S(2)}, u32[]{:S(2)}) collective-permute-start(bf16[96,576]{1,0:T(8,128)(2,1)S(1)} %collective-permute-done.11), channel_id=1, source_target_pairs={{8,0},{16,8},{24,16},{32,24},{40,32},{48,40},{56,48},{64,56},{72,6... | collective-permute-start | bytes 331784 | tf_op jit(solution)/shard_map/ppermute | solution.py:27
  277.1 7.9 %collective-permute-start.6 = (bf16[96,576]{1,0:T(8,128)(2,1)S(1)}, bf16[96,576]{1,0:T(8,128)(2,1)S(1)}, u32[]{:S(2)}, u32[]{:S(2)}) collective-permute-start(bf16[96,576]{1,0:T(8,128)(2,1)S(1)} %collective-permute-done.5), channel_id=1, source_target_pairs={{0,8},{8,16},{16,24},{24,32},{32,40},{40,48},{48,56},{56,64},{64,7... | collective-permute-start | bytes 331784 | tf_op jit(solution)/shard_map/ppermute | solution.py:25
  277.1 7.9 %collective-permute-start.13 = (bf16[96,576]{1,0:T(8,128)(2,1)S(1)}, bf16[96,576]{1,0:T(8,128)(2,1)S(1)}, u32[]{:S(2)}, u32[]{:S(2)}) collective-permute-start(bf16[96,576]{1,0:T(8,128)(2,1)S(1)} %collective-permute-done.12), channel_id=1, source_target_pairs={{8,0},{16,8},{24,16},{32,24},{40,32},{48,40},{56,48},{64,56},{72,6... | collective-permute-start | bytes 331784 | tf_op jit(solution)/shard_map/ppermute | solution.py:27
  284.9 7.1 %collective-permute-start.7 = (bf16[96,576]{1,0:T(8,128)(2,1)S(1)}, bf16[96,576]{1,0:T(8,128)(2,1)S(1)}, u32[]{:S(2)}, u32[]{:S(2)}) collective-permute-start(bf16[96,576]{1,0:T(8,128)(2,1)S(1)} %collective-permute-done.6), channel_id=1, source_target_pairs={{0,8},{8,16},{16,24},{24,32},{32,40},{40,48},{48,56},{56,64},{64,7... | collective-permute-start | bytes 331784 | tf_op jit(solution)/shard_map/ppermute | solution.py:25
  285.0 16.9 %collective-permute-start.14 = (bf16[96,576]{1,0:T(8,128)(2,1)S(1)}, bf16[96,576]{1,0:T(8,128)(2,1)S(1)}, u32[]{:S(2)}, u32[]{:S(2)}) collective-permute-start(bf16[96,576]{1,0:T(8,128)(2,1)S(1)} %collective-permute-done.13), channel_id=1, source_target_pairs={{8,0},{16,8},{24,16},{32,24},{40,32},{48,40},{56,48},{64,56},{72,6... | collective-permute-start | bytes 331784 | tf_op jit(solution)/shard_map/ppermute | solution.py:27
  340.5 44.2 %copy-start.1 = (bf16[1536,256]{1,0:T(8,128)(2,1)S(1)}, bf16[1536,256]{1,0:T(8,128)(2,1)}, u32[]{:S(2)}) copy-start(bf16[1536,256]{1,0:T(8,128)(2,1)} %param.17) | copy-start | bytes 2359300
  (11 other events, 72.9 us)
Sparse Core Ops, SparseCore 0:
  19.9 26.9 all-gather.4
  49.3 139.3 all-gather.8
  233.8 45.4 all-gather.6
  281.3 43.6 all-gather.10
  340.6 41.8 reduce-scatter.1
